TPU v7x, 32 devices: a whole 2x2x4 slice. The times are simulated.
32 devices in a mesh: freq: 4 (over y, core), row: 8 (over z, x).
Axes of the slice: x: 2, y: 2, z: 4, core: 2. Of those that a mesh axis runs over, the one named last changes fastest.
Arguments:
- traces: bfloat16 [2, 8192, 8192], P(None, ('freq', 'row')), may hold values from -1.1953125 to 1.1953125
- prior: bfloat16 [4, 2, 8192, 8192], P('freq', None, None, 'row'), may hold values from -0.796875 to 0.796875
- bins: int32 [4], replicated, may hold values from 64 to 255
- panels: int32 [2], replicated, may hold values from 0 to 31
Outputs:
- multiples: bfloat16 [4, 2, 8192, 8192], P('freq', None, 'row')
- spectrum: bfloat16 [4, 2, 8192, 8192], P('freq', None, None, 'row')
All inputs are finite; a program needn't handle non-finite values.
Results may differ from a plain program's by a relative error of at most 0.0077.
Values may be sent and summed in bfloat16 or wider, within the bound.
No kernel may reach another device: no remote copies, remote signals or barrier semaphores. Data moves between devices by JAX's collectives and lax.ppermute only.
A program may use at most 640 MiB of HBM per device.

v0:
```python
import math
import jax
import jax.numpy as jnp
from jax import lax
from jax.sharding import PartitionSpec as P

NT_REC = 1024
PANEL = 256
STEPS = 2
BLOCK_START = 1022


def spread(value, axis, source):
    kept = jnp.where(lax.axis_index(axis) == source, value, 0).astype(value.dtype)
    return lax.psum(kept, axis)


def complex_terms(left, right):
    dims = (((0,), (1,)), ((), ()))

    def product(first, second):
        return lax.dot_general(first, second, dims, preferred_element_type=jnp.float32)

    real_part = product(left[0], right[0]) - product(left[1], right[1])
    imag_part = product(left[0], right[1]) + product(left[1], right[0])
    return (real_part, imag_part)


def body(traces, prior, bins, panels):
    sample_count, shots_local, receivers = traces.shape
    row_count = lax.axis_size("row")
    block_rows = receivers // row_count
    sample_index = BLOCK_START + jnp.arange(sample_count, dtype=jnp.int32)
    turn_count = bins[:, None] * sample_index[None, :] % NT_REC
    angles = 2.0 * math.pi / NT_REC * turn_count.astype(jnp.float32)
    twiddle = jnp.stack([jnp.cos(angles), -jnp.sin(angles)], axis=1).astype(jnp.bfloat16)
    own_twiddle = lax.dynamic_index_in_dim(twiddle, lax.axis_index("freq"), 0, keepdims=False)
    by_row = lax.all_to_all(traces, "row", split_axis=2, concat_axis=1, tiled=True)
    gathered = lax.all_gather(by_row, "freq", axis=1, tiled=True)
    transformed = jnp.einsum(
        "tsb,ct->csb", gathered, own_twiddle, preferred_element_type=jnp.float32
    ).astype(jnp.bfloat16)
    spectrum = (prior[0].astype(jnp.float32) + transformed.astype(jnp.float32)).astype(jnp.bfloat16)
    panels_each = block_rows // PANEL
    real_sum = jnp.zeros((block_rows, receivers), jnp.float32)
    imag_sum = jnp.zeros((block_rows, receivers), jnp.float32)
    for panel_step in range(STEPS):
        chosen = panels[panel_step]
        owner = chosen // panels_each
        offset = chosen % panels_each * PANEL
        own_rows = lax.dynamic_slice_in_dim(spectrum, offset, PANEL, 2)
        panel_data = spread(own_rows, "row", owner)
        left = lax.dynamic_slice_in_dim(spectrum, chosen * PANEL, PANEL, 1)
        real_part, imag_part = complex_terms(left, panel_data)
        real_sum = real_sum + real_part
        imag_sum = imag_sum + imag_part
    return (jnp.stack([real_sum, imag_sum])[None].astype(jnp.bfloat16), spectrum[None])


def solution(mesh):
    return jax.shard_map(
        body,
        mesh=mesh,
        in_specs=(P(None, ("freq", "row"), None), P("freq", None, None, "row"), P(), P()),
        out_specs=(P("freq", None, "row", None), P("freq", None, None, "row")),
        check_vma=False,
    )
```

profile of v0, /device:TPU:0, one launch (start us, length us, event | category | flops | bytes accessed | tf_op | source)
XLA Modules:
  0.0 1370.1 jit_solution(301745803882222178)
XLA Ops:
  7.2 21.0 %copy.21 = bf16[2,256,8192]{1,0,2:T(2,128)(2,1)} copy(bf16[2,256,8192]{2,1,0:T(8,128)(2,1)} %param.4) | data formatting | bytes 16777216 | tf_op args[0]
  28.2 190.4 %all_to_all.18 = bf16[2,256,8192]{1,0,2:T(2,128)(2,1)} all-to-all(bf16[2,256,8192]{1,0,2:T(2,128)(2,1)} %copy.21), channel_id=1, replica_groups=mesh['freq'=4,'row'=8] {'row'}, dimensions={2} | all-to-all | bytes 16777216 | tf_op jit(solution)/shard_map/all_to_all | solution.py:38
  218.6 30.5 %copy.22 = bf16[2,8,256,1024]{3,0,2,1:T(2,128)(2,1)} copy(bf16[2,8,256,1024]{2,0,3,1:T(2,128)(2,1)} %bitcast.60) | data formatting | bytes 16777216 | tf_op jit(solution)/shard_map/all_to_all | solution.py:38
  249.1 0.0 all-reduce.3.cloned.1.call-start
  249.2 0.6 copy-done.1
  249.8 0.6 fusion.49
  255.3 0.1 cosine_convert_fusion
  255.4 0.2 fusion.45
  255.6 194.4 %all-gather.2.cloned.1.call-done = bf16[2,8192,1024]{2,0,1:T(2,128)(2,1)} async-done(((bf16[2,2048,1024]{2,0,1:T(2,128)(2,1)}), bf16[2,8192,1024]{2,0,1:T(2,128)(2,1)}) %all-gather.2.cloned.1.call-update) | async-done | bytes 33554448 | tf_op jit(solution)/shard_map/all_gather | solution.py:39
  449.9 145.3 %fusion = bf16[2,8192,1024]{2,0,1:T(2,128)(2,1)} fusion(bf16[1,2,8192,1024]{3,2,1,0:T(8,128)(2,1)} %param.5, bf16[2,8192,1024]{2,0,1:T(2,128)(2,1)} %all-gather.2.cloned.1.call-done, bf16[2,2]{1,0:T(2,128)(2,1)S(1)} %fusion.45), kind=kOutput, calls=%fused_computation.1 | convolution fusion | flops 150994944 | bytes 100663304 | tf_op jit(solution)/shard_map/tsb,ct->csb/dot_general | solution.py:40
  595.3 17.1 %broadcast_select_fusion.1 = (bf16[2,8192,256]{2,0,1:T(2,128)(2,1)}, bf16[2,8192,256]{2,0,1:T(2,128)(2,1)}) fusion(pred[]{:T(512)S(6)} %eq.11, bf16[2,8192,1024]{2,0,1:T(2,128)(2,1)} %fusion, s32[]{:T(128)S(6)} %select_n.71, s32[]{:T(128)S(6)} %select_n.77, pred[]{:T(512)S(6)} %eq.12), kind=kLoop, calls=%fused_computation.7 | loop fusion | flops 8388608 | bytes 33554440 | tf_op jit(solution)/shard_map/jit(_where)/select_n | solution.py:14
  613.6 23.4 %copy.23 = bf16[1,2,8192,1024]{3,2,1,0:T(8,128)(2,1)} copy(bf16[1,2,8192,1024]{3,1,2,0:T(2,128)(2,1)} %bitcast.58) | data formatting | bytes 67108864
  637.0 6.3 constant_dynamic-slice_fusion.3
  643.3 479.6 %all-reduce.3.cloned.1.call-done = (bf16[2,8192,256]{2,0,1:T(2,128)(2,1)}, bf16[2,8192,256]{2,0,1:T(2,128)(2,1)}) async-done(((bf16[2,8192,256]{2,0,1:T(2,128)(2,1)}, bf16[2,8192,256]{2,0,1:T(2,128)(2,1)}), (bf16[2,8192,256]{2,0,1:T(2,128)(2,1)}, bf16[2,8192,256]{2,0,1:T(2,128)(2,1)})) %all-reduce.3.cloned.1.call-update) | async-done | bytes 16777232 | tf_op jit(solution)/shard_map/psum | solution.py:15
  1122.9 33.0 %fusion.47 = (bf16[1,8192,256]{2,0,1:T(2,128)(2,1)}, bf16[1,8192,256]{2,0,1:T(2,128)(2,1)}, bf16[1,8192,256]{2,0,1:T(2,128)(2,1)}, bf16[1,8192,256]{2,0,1:T(2,128)(2,1)}) fusion(bf16[2,8192,256]{2,0,1:T(2,128)(2,1)} %get-tuple-element.12, bf16[2,8192,256]{2,0,1:T(2,128)(2,1)} %get-tuple-element.13), kind=kLoop, calls=%fused_computation.67 | loop fusion | bytes 33554432 | tf_op jit(solution)/shard_map/slice | solution.py:24
  1155.9 19.5 %fusion.11 = f32[1024,8192]{1,0:T(8,128)} fusion(bf16[1,8192,256]{2,0,1:T(2,128)(2,1)} %get-tuple-element.28, bf16[1,256,1024]{2,0,1:T(2,128)(2,1)} %get-tuple-element.17), kind=kOutput, calls=%fused_computation.18 | convolution fusion | flops 4294967296 | bytes 38273024 | tf_op jit(solution)/shard_map/dot_general | solution.py:22
  1175.3 16.5 %fusion.13 = f32[1024,8192]{1,0:T(8,128)} fusion(bf16[1,8192,256]{2,0,1:T(2,128)(2,1)} %get-tuple-element.29, bf16[1,256,1024]{2,0,1:T(2,128)(2,1)S(1)} %copy-done), kind=kOutput, calls=%fused_computation.20 | convolution fusion | flops 4294967296 | bytes 38273024 | tf_op jit(solution)/shard_map/dot_general | solution.py:22
  1191.9 16.5 %fusion.15 = f32[1024,8192]{1,0:T(8,128)} fusion(bf16[1,8192,256]{2,0,1:T(2,128)(2,1)} %get-tuple-element.29, bf16[1,256,1024]{2,0,1:T(2,128)(2,1)S(1)} %get-tuple-element.16), kind=kOutput, calls=%fused_computation.22 | convolution fusion | flops 4294967296 | bytes 38273024 | tf_op jit(solution)/shard_map/dot_general | solution.py:22
  1208.4 16.5 %fusion.9 = f32[1024,8192]{1,0:T(8,128)} fusion(bf16[1,8192,256]{2,0,1:T(2,128)(2,1)} %get-tuple-element.28, bf16[1,256,1024]{2,0,1:T(2,128)(2,1)S(1)} %get-tuple-element.16), kind=kOutput, calls=%fused_computation.16 | convolution fusion | flops 4294967296 | bytes 38273024 | tf_op jit(solution)/shard_map/dot_general | solution.py:22
  1225.0 16.5 %fusion.7 = f32[1024,8192]{1,0:T(8,128)} fusion(bf16[1,8192,256]{2,0,1:T(2,128)(2,1)} %get-tuple-element.20, bf16[1,256,1024]{2,0,1:T(2,128)(2,1)S(1)} %get-tuple-element.15), kind=kOutput, calls=%fused_computation.14 | convolution fusion | flops 4294967296 | bytes 38273024 | tf_op jit(solution)/shard_map/dot_general | solution.py:22
  1241.5 17.5 %fusion.3 = f32[1024,8192]{1,0:T(8,128)} fusion(bf16[1,8192,256]{2,0,1:T(2,128)(2,1)} %get-tuple-element.21, bf16[1,256,1024]{2,0,1:T(2,128)(2,1)S(1)} %get-tuple-element.15), kind=kOutput, calls=%fused_computation.10 | convolution fusion | flops 4294967296 | bytes 38273024 | tf_op jit(solution)/shard_map/dot_general | solution.py:22
  1259.0 40.7 %fusion.1 = bf16[1,1,1024,8192]{3,2,1,0:T(8,128)(2,1)} fusion(f32[1024,8192]{1,0:T(8,128)} %fusion.7, f32[1024,8192]{1,0:T(8,128)} %fusion.15, f32[1024,8192]{1,0:T(8,128)} %fusion.11, bf16[1,8192,256]{2,0,1:T(2,128)(2,1)} %get-tuple-element.21, bf16[1,256,1024]{2,0,1:T(2,128)(2,1)S(1)} %get-tuple-element.14), kind=kOutput, calls=%fused_computation.8 | convolution fusion | flops 4328521728 | bytes 122159104 | tf_op jit(solution)/shard_map/dot_general | solution.py:22
  1299.7 40.6 %fusion.2 = bf16[1,1,1024,8192]{3,2,1,0:T(8,128)(2,1)} fusion(f32[1024,8192]{1,0:T(8,128)} %fusion.3, f32[1024,8192]{1,0:T(8,128)} %fusion.9, f32[1024,8192]{1,0:T(8,128)} %fusion.13, bf16[1,8192,256]{2,0,1:T(2,128)(2,1)} %get-tuple-element.20, bf16[1,256,1024]{2,0,1:T(2,128)(2,1)S(1)} %get-tuple-element.14), kind=kOutput, calls=%fused_computation.9 | convolution fusion | flops 4328521728 | bytes 122159104 | tf_op jit(solution)/shard_map/dot_general | solution.py:22
  1340.3 23.0 %pad_maximum_fusion = bf16[1,2,1024,8192]{3,2,1,0:T(8,128)(2,1)} fusion(bf16[1,1,1024,8192]{3,2,1,0:T(8,128)(2,1)} %fusion.2, bf16[1,1,1024,8192]{3,2,1,0:T(8,128)(2,1)} %fusion.1), kind=kLoop, calls=%fused_computation.3 | loop fusion | flops 16777216 | bytes 67108864 | tf_op jit(solution)/shard_map/stack | solution.py:57
  (9 shorter events, 0.1 us)
Async XLA Ops:
  7.2 442.8 %all-gather.2.cloned.1.call-start = ((), (), s32[]{:S(2)}) async-start(), calls=%async_computation.1 | async-start | bytes 41943040 | tf_op jit(solution)/shard_map/all_gather | solution.py:39
  249.1 0.7 copy-start.1
  249.1 6.2 copy-start.2
  249.1 873.8 %all-reduce.3.cloned.1.call-start = ((), (), s32[]{:S(2)}) async-start(), calls=%async_computation.2 | async-start | bytes 33554432 | tf_op jit(solution)/shard_map/psum | solution.py:15
  1155.9 19.5 %copy-start = (bf16[1,256,1024]{2,0,1:T(2,128)(2,1)S(1)}, bf16[1,256,1024]{2,0,1:T(2,128)(2,1)}, u32[]{:S(2)}) copy-start(bf16[1,256,1024]{2,0,1:T(2,128)(2,1)} %get-tuple-element.17) | copy-start | bytes 1572868
Sparse Core Ops, SparseCore 0:
  249.2 200.6 all-gather.1
  612.5 510.3 all-reduce.2
where the time goes:
time: 1370 us
  waiting for transfers between devices  674 us (49%)
  matrix products  330 us (24%)
  blocking collectives  190 us (14%)
  local copies, waits for them, and re-layouts  115 us (8%)
  other arithmetic  40.3 us (3%)
  between operations  20.2 us (1%)
    psum x1, waiting for transfers between devices, spread(): return lax.psum(kept, axis)  480 us
    all_gather x1, waiting for transfers between devices, body(): gathered = lax.all_gather(by_row, 'freq', axis=1, tiled=True)  194 us
    all_to_all x1, blocking collectives, body(): lax.all_to_all(traces, 'row', split_axis=2, concat_axis=1, tiled=True)  190 us
    dot_general x8, matrix products, product(): lax.dot_general(first, second, dims, preferred_element_type=jnp.float32)  184 us
    dot_general x1, matrix products, body(): jnp.einsum('tsb,ct->csb', gathered, own_twiddle, preferred_element_type=j...  145 us
    unnamed x8, local copies, waits for them, and re-layouts  45 us
    slice x2, local copies, waits for them, and re-layouts, complex_terms(): real_part = product(left[0], right[0]) - product(left[1], right[1])  39.3 us
    all_to_all x1, local copies, waits for them, and re-layouts, body(): lax.all_to_all(traces, 'row', split_axis=2, concat_axis=1, tiled=True)  30.5 us
  transfers between devices with their start and end apart: 2, of which 2 were waited for; matrix products, arithmetic and copies ran while one was open for 2% of the time, Pallas kernels for 0%

commit v1 on v0

--- a/solution.py
+++ b/solution.py
@@ -12,7 +12,7 @@
 
 def spread(value, axis, source):
     kept = jnp.where(lax.axis_index(axis) == source, value, 0).astype(value.dtype)
-    return lax.psum(kept, axis)
+    return jnp.sum(lax.all_gather(kept, axis), axis=0)
 
 
 def complex_terms(left, right):

time: 1370 us -> 3360 us (2.45)
  waiting for transfers between devices: 674 us -> 2630 us
  other arithmetic: 40.3 us -> 94.8 us
    all_gather x0 -> x2, waiting for transfers between devices: none -> 2430 us  [spread(): return jnp.sum(lax.all_gather(kept, axis), axis=0)]
    psum x1 -> x0, waiting for transfers between devices: 480 us -> none  [spread(): return lax.psum(kept, axis)]
    reduce_sum x0 -> x2, other arithmetic: none -> 54.5 us  [spread(): return jnp.sum(lax.all_gather(kept, axis), axis=0)]
  transfers between devices with their start and end apart: 2 -> 3, of which waited for: 2 -> 3; matrix products, arithmetic and copies ran while one was open for 2% -> 3% of each run, Pallas kernels for 0% -> 0%
where the time goes in v1:
time: 3360 us; the launch traced here: 3350 us
  waiting for transfers between devices  2630 us (78%)
  matrix products  320 us (10%)
  blocking collectives  190 us (6%)
  local copies, waits for them, and re-layouts  97.7 us (3%)
  other arithmetic  94.8 us (3%)
    all_gather x2, waiting for transfers between devices, spread(): return jnp.sum(lax.all_gather(kept, axis), axis=0)  2430 us
    all_gather x1, waiting for transfers between devices, body(): gathered = lax.all_gather(by_row, 'freq', axis=1, tiled=True)  195 us
    all_to_all x1, blocking collectives, body(): lax.all_to_all(traces, 'row', split_axis=2, concat_axis=1, tiled=True)  190 us
    dot_general x8, matrix products, product(): lax.dot_general(first, second, dims, preferred_element_type=jnp.float32)  175 us
    dot_general x1, matrix products, body(): jnp.einsum('tsb,ct->csb', gathered, own_twiddle, preferred_element_type=j...  145 us
  transfers between devices with their start and end apart: 3, of which 3 were waited for; matrix products, arithmetic and copies ran while one was open for 3% of the time, Pallas kernels for 0%

profile of v1, /device:TPU:0, one launch (start us, length us, event | category | flops | bytes accessed | tf_op | source)
XLA Modules:
  0.0 3351.6 jit_solution(6603935982501079159)
XLA Ops:
  7.2 21.0 copy.37
  28.2 190.4 %all_to_all.18 = bf16[2,256,8192]{1,0,2:T(2,128)(2,1)} all-to-all(bf16[2,256,8192]{1,0,2:T(2,128)(2,1)} %copy.37), channel_id=1, replica_groups=mesh['freq'=4,'row'=8] {'row'}, dimensions={2} | all-to-all | bytes 16777216 | tf_op jit(solution)/shard_map/all_to_all | solution.py:38
  218.6 30.5 copy.38
  249.2 0.6 fusion.31
  255.3 194.8 %all-gather.6.cloned.1.call-done = bf16[2,8192,1024]{2,0,1:T(2,128)(2,1)} async-done(((bf16[2,2048,1024]{2,0,1:T(2,128)(2,1)}), bf16[2,8192,1024]{2,0,1:T(2,128)(2,1)}) %all-gather.6.cloned.1.call-update) | async-done | bytes 33554448 | tf_op jit(solution)/shard_map/all_gather | solution.py:39
  450.1 145.3 %fusion = bf16[2,8192,1024]{2,0,1:T(2,128)(2,1)} fusion(bf16[1,2,8192,1024]{3,2,1,0:T(8,128)(2,1)} %param.5, bf16[2,8192,1024]{2,0,1:T(2,128)(2,1)} %all-gather.6.cloned.1.call-done, bf16[2,2]{1,0:T(2,128)(2,1)S(1)} %fusion.29), kind=kOutput, calls=%fused_computation.1 | convolution fusion | flops 150994944 | bytes 100663304 | tf_op jit(solution)/shard_map/tsb,ct->csb/dot_general | solution.py:40
  595.4 17.1 broadcast_select_fusion.1
  612.5 7.7 copy.41
  620.7 8.1 copy.39
  630.1 23.4 copy.43
  653.5 6.4 constant_dynamic-slice_fusion.3
  659.9 1227.3 %all-gather.10.cloned.1.call-done = bf16[16,8192,256]{2,1,0:T(8,128)(2,1)} async-done(((bf16[2,8192,256]{2,1,0:T(8,128)(2,1)}), bf16[16,8192,256]{2,1,0:T(8,128)(2,1)}) %all-gather.10.cloned.1.call-update) | async-done | bytes 67108880 | tf_op jit(solution)/shard_map/all_gather | solution.py:15
  1887.1 28.6 reduce_sum.25
  1915.8 18.9 fusion.8
  1934.7 15.6 fusion.7
  1950.3 1205.3 %all-gather.8.cloned.1.call-done = bf16[16,8192,256]{2,1,0:T(8,128)(2,1)} async-done(((bf16[2,8192,256]{2,1,0:T(8,128)(2,1)}), bf16[16,8192,256]{2,1,0:T(8,128)(2,1)}) %all-gather.8.cloned.1.call-update) | async-done | bytes 67108880 | tf_op jit(solution)/shard_map/all_gather | solution.py:15
  3155.6 25.8 reduce_sum.24
  3181.4 15.3 fusion.5
  3196.8 15.3 fusion.4
  3212.1 15.5 fusion.3
  3227.6 15.3 fusion.6
  3243.0 39.5 %fusion.2 = bf16[1,1,1024,8192]{3,2,1,0:T(8,128)(2,1)} fusion(f32[1024,8192]{1,0:T(8,128)} %fusion.8, f32[1024,8192]{1,0:T(8,128)} %fusion.5, f32[1024,8192]{1,0:T(8,128)} %fusion.3, bf16[2,8192,256]{2,1,0:T(8,128)(2,1)} %reduce_sum.25, bf16[1,256,1024]{2,0,1:T(2,128)(2,1)S(1)} %get-tuple-element.14), kind=kOutput, calls=%fused_computation.9 | convolution fusion | flops 4328521728 | bytes 122159104 | tf_op jit(solution)/shard_map/dot_general | solution.py:22
  3282.4 39.4 %fusion.1 = bf16[1,1,1024,8192]{3,2,1,0:T(8,128)(2,1)} fusion(f32[1024,8192]{1,0:T(8,128)} %fusion.7, f32[1024,8192]{1,0:T(8,128)} %fusion.4, f32[1024,8192]{1,0:T(8,128)} %fusion.6, bf16[2,8192,256]{2,1,0:T(8,128)(2,1)} %reduce_sum.25, bf16[1,256,1024]{2,0,1:T(2,128)(2,1)S(1)} %get-tuple-element.14), kind=kOutput, calls=%fused_computation.8 | convolution fusion | flops 4328521728 | bytes 122159104 | tf_op jit(solution)/shard_map/dot_general | solution.py:22
  3321.9 23.0 pad_maximum_fusion
  (15 shorter events, 0.9 us)
Async XLA Ops:
  7.2 442.9 %all-gather.6.cloned.1.call-start = ((), (), s32[]{:S(2)}) async-start(), calls=%async_computation.1 | async-start | bytes 41943040 | tf_op jit(solution)/shard_map/all_gather | solution.py:39
  218.6 30.6 copy-start.1
  218.6 36.3 %copy-start.2 = (s32[4]{0:T(128)S(1)}, s32[4]{0:T(128)}, u32[]{:S(2)}) copy-start(s32[4]{0:T(128)} %param.6) | copy-start | bytes 52
  249.2 1638.0 %all-gather.10.cloned.1.call-start = ((), (), s32[]{:S(2)}) async-start(), calls=%async_computation.3 | async-start | bytes 75497472 | tf_op jit(solution)/shard_map/all_gather | solution.py:15
  620.2 2535.4 %all-gather.8.cloned.1.call-start = ((), (), s32[]{:S(2)}) async-start(), calls=%async_computation.2 | async-start | bytes 75497472 | tf_op jit(solution)/shard_map/all_gather | solution.py:15
  1915.8 18.9 copy-start
Sparse Core Ops, SparseCore 0:
  249.3 200.7 all-gather.5
  620.3 1266.7 all-gather.9
  1888.7 1266.8 all-gather.7
